TPU v7x, 256 devices: a whole 4x4x8 slice. The times are simulated.
256 devices in a mesh: seq: 8 (over x, core), vocab: 32 (over z, y).
Axes of the slice: x: 4, y: 4, z: 8, core: 2. Of those that a mesh axis runs over, the one named last changes fastest.
Arguments:
- hidden: bfloat16 [2048, 4096], P('seq'), may hold values from -48 to 48
- head_weight: bfloat16 [4096, 65536], P('seq', 'vocab'), may hold values from -0.09375 to 0.09375
- queries: float32 [16, 65536], P(None, 'vocab'), may hold values from 0 to 1, as said below
- passage_lengths: int32 [32], replicated, may hold values from 1 to 192, 2048 in all
- pairing: int32 [32], replicated, may hold values from 0 to 15
- doc_freq: int32 [65536], P('vocab'), may hold values from 0 to 4194304
Outputs:
- grad_hidden: bfloat16 [2048, 4096], P('seq', 'vocab')
- losses: float32 [2], replicated
Inputs may be any that keep to these rules, and one draw needn't show every extreme that they name: `queries`: entries are nonnegative.
All inputs are finite; a program needn't handle non-finite values.
Results may differ from a plain program's by a relative error of at most 0.0039.
Values may be sent and summed in bfloat16 or wider, within the bound.
No kernel may reach another device: no remote copies, remote signals or barrier semaphores. Data moves between devices by JAX's collectives and lax.ppermute only.
A program may use at most 128 MiB of HBM per device.

v0:
```python
import jax
import jax.numpy as jnp
from jax import lax
from jax.sharding import Mesh, PartitionSpec as P

DOCS = 4194304
sharpness = 8.0
loss_scale = 16384.0
flops_weight = 32.0
highest = lax.Precision.HIGHEST
SEQ = ("sx", "sc")
VOC = ("vz", "vy")
GROUPS = 2


def butterfly(x, axes_sizes):
    for ax, n in axes_sizes:
        d = 1
        while d < n:
            x = jax.tree.map(lambda a: a + lax.ppermute(a, ax, [(i, i ^ d) for i in range(n)]), x)
            d *= 2
    return x


def halving_scatter(x, ax, n):
    me = lax.axis_index(ax)
    d = n // 2
    while d >= 1:
        h = x.shape[0] // 2
        bit = me // d % 2
        keep = lax.dynamic_slice_in_dim(x, bit * h, h, 0)
        send = lax.dynamic_slice_in_dim(x, (1 - bit) * h, h, 0)
        x = keep + lax.ppermute(send, ax, [(i, i ^ d) for i in range(n)])
        d //= 2
    return x


def softmax_terms(scores, pair_rows):
    onehot = (jnp.arange(scores.shape[0], dtype=jnp.int32)[:, None] == pair_rows[None, :]).astype(
        jnp.float32
    )
    peak_score = jnp.max(scores, axis=0)
    shifted = jnp.exp(scores - peak_score[None, :])
    denominator = jnp.sum(shifted, axis=0)
    log_total = peak_score + jnp.log(denominator)
    losses_each = log_total - jnp.sum(onehot * scores, axis=0)
    return (losses_each, shifted / denominator[None, :] - onehot)


def per_device(sizes, hidden, head_weight, queries, passage_lengths, pairing, doc_freq):
    n_sx, n_sc, n_vz, n_vy = sizes
    tok_rows = hidden.shape[0]
    vocab_cols = head_weight.shape[1]
    passages = passage_lengths.shape[0]
    vocab_total = vocab_cols * n_vz * n_vy
    finish = jnp.cumsum(passage_lengths)
    starts = finish - passage_lengths
    seq_index = lax.axis_index("sx") * n_sc + lax.axis_index("sc")
    position = seq_index * tok_rows + jnp.arange(tok_rows, dtype=jnp.int32)
    member = (
        (position[None, :] >= starts[:, None]) & (position[None, :] < finish[:, None])
    ).astype(jnp.float32)
    counts = passage_lengths.astype(jnp.float32)
    weights_df = jnp.log(1.0 + DOCS / (1.0 + doc_freq.astype(jnp.float32)))
    flops_grad = loss_scale * flops_weight * 2.0 / (vocab_total * passages)
    full_head = lax.all_gather(head_weight, SEQ, axis=0, tiled=True)
    logits = jnp.dot(hidden, full_head, preferred_element_type=jnp.float32)
    lifted = 1.0 + jax.nn.relu(logits)
    squared = lifted * lifted
    fourth = squared * squared
    powered = fourth * fourth
    local_sums = jnp.dot(member, powered, precision=highest)
    totals = butterfly(local_sums, [("sc", n_sc), ("sx", n_sx)])
    pooled = (jnp.log(totals) - jnp.log(counts)[:, None]) / sharpness
    col_mean = jnp.sum(pooled, axis=0) / passages
    flops_part = jnp.sum(weights_df * col_mean * col_mean) / vocab_total
    score_part = jnp.dot(queries, pooled.T, precision=highest)
    flops_row = jnp.where(jnp.arange(passages) == 0, flops_part, 0.0)[None, :]
    summed = butterfly(
        jnp.concatenate([score_part, flops_row], axis=0), [("vy", n_vy), ("vz", n_vz)]
    )
    scores, flops_value = (summed[:-1], summed[-1, 0])
    losses_each, probs = softmax_terms(scores, pairing)
    contrast = jnp.mean(losses_each)
    dscores = probs * (loss_scale / passages)
    dpooled = jnp.dot(dscores.T, queries, precision=highest) + flops_grad * weights_df * col_mean
    factor = dpooled / totals
    spread = lax.dot_general(member, factor, (((0,), (0,)), ((), ())), precision=highest)
    seventh = fourth * squared * lifted
    dlogits = jnp.where(logits > 0, spread * seventh, 0.0).astype(jnp.bfloat16)
    n_out = n_vz * n_vy
    width = full_head.shape[0] // n_out
    grouped = full_head.reshape(n_out, GROUPS, width // GROUPS, vocab_cols)
    pieces = []
    for g in range(GROUPS):
        rows = grouped[:, g].reshape(-1, vocab_cols)
        partial = lax.dot_general(
            rows, dlogits, (((1,), (1,)), ((), ())), preferred_element_type=jnp.float32
        )
        pieces.append(
            halving_scatter(
                lax.psum_scatter(partial, "vz", scatter_dimension=0, tiled=True), "vy", n_vy
            )
        )
    grad_cols = jnp.concatenate(pieces, axis=0)
    losses = jnp.stack([contrast, flops_value])
    return (grad_cols.T.astype(jnp.bfloat16), losses)


def solution(mesh):
    n_seq, n_voc = mesh.devices.shape
    n_sc = 2
    n_vy = 4
    sizes = (n_seq // n_sc, n_sc, n_voc // n_vy, n_vy)
    mesh4 = Mesh(mesh.devices.reshape(sizes), ("sx", "sc", "vz", "vy"))
    placed = (P(SEQ, None), P(SEQ, VOC), P(None, VOC), P(), P(), P(VOC))
    return jax.shard_map(
        lambda *a: per_device(sizes, *a),
        mesh=mesh4,
        in_specs=placed,
        out_specs=(P(SEQ, VOC), P()),
        check_vma=False,
    )
```

profile of v0, /device:TPU:10, one launch (start us, length us, event | category | flops | bytes accessed | tf_op | source)
XLA Modules:
  0.0 275.6 jit_solution(13790768649974117661)
XLA Ops:
  8.3 91.5 %all-gather.2.cloned.1.call-done = bf16[4096,2048]{1,0:T(8,128)(2,1)} async-done(((bf16[512,2048]{1,0:T(8,128)(2,1)}), bf16[4096,2048]{1,0:T(8,128)(2,1)}) %all-gather.2.cloned.1.call-update) | async-done | bytes 16777232 | tf_op jit(solution)/shard_map/all_gather | solution.py:66
  99.8 8.1 %fusion.34 = f32[256,2048]{1,0:T(8,128)S(1)} fusion(bf16[256,4096]{1,0:T(8,128)(2,1)S(1)} %copy-done, bf16[4096,2048]{1,0:T(8,128)(2,1)} %all-gather.2.cloned.1.call-done), kind=kOutput, calls=%fused_computation.66 | convolution fusion | flops 4294967296 | bytes 20971520 | tf_op jit(solution)/shard_map/dot_general | solution.py:67
  109.5 1.3 collective-permute-done
  111.8 7.6 %collective-permute-done.1 = f32[32,2048]{1,0:T(8,128)S(1)} collective-permute-done((f32[32,2048]{1,0:T(8,128)S(1)}, f32[32,2048]{1,0:T(8,128)S(1)}, u32[]{:S(2)}, u32[]{:S(2)}) %collective-permute-start.1) | collective-permute-done | bytes 262176 | tf_op jit(solution)/shard_map/ppermute | solution.py:20
  120.7 7.9 %collective-permute-done.2 = f32[32,2048]{1,0:T(8,128)S(1)} collective-permute-done((f32[32,2048]{1,0:T(8,128)S(1)}, f32[32,2048]{1,0:T(8,128)S(1)}, u32[]{:S(2)}, u32[]{:S(2)}) %collective-permute-start.2) | collective-permute-done | bytes 262176 | tf_op jit(solution)/shard_map/ppermute | solution.py:20
  131.1 3.2 %collective-permute-done.3 = f32[17,32]{1,0:T(8,128)S(1)} collective-permute-done((f32[17,32]{1,0:T(8,128)S(1)}, f32[17,32]{1,0:T(8,128)S(1)}, u32[]{:S(2)}, u32[]{:S(2)}) %collective-permute-start.3) | collective-permute-done | bytes 2208 | tf_op jit(solution)/shard_map/ppermute | solution.py:20
  134.3 2.1 collective-permute-start.4
  136.4 3.1 %collective-permute-done.4 = f32[17,32]{1,0:T(8,128)S(1)} collective-permute-done((f32[17,32]{1,0:T(8,128)S(1)}, f32[17,32]{1,0:T(8,128)S(1)}, u32[]{:S(2)}, u32[]{:S(2)}) %collective-permute-start.4) | collective-permute-done | bytes 2208 | tf_op jit(solution)/shard_map/ppermute | solution.py:20
  139.5 1.6 collective-permute-start.5
  141.0 2.1 collective-permute-done.5
  143.2 2.5 collective-permute-start.6
  145.7 2.1 collective-permute-done.6
  147.8 5.8 %collective-permute-start.7 = (f32[17,32]{1,0:T(8,128)S(1)}, f32[17,32]{1,0:T(8,128)S(1)}, u32[]{:S(2)}, u32[]{:S(2)}) collective-permute-start(f32[17,32]{1,0:T(8,128)S(1)} %add.116), channel_id=1, source_target_pairs={{0,16},{4,20},{8,24},{12,28},{16,0},{20,4},{24,8},{28,12},{1,17},{... | collective-permute-start | bytes 6536 | tf_op jit(solution)/shard_map/ppermute | solution.py:20
  153.5 9.9 %fusion.33 = (bf16[32,1,64,2048]{3,2,1,0:T(8,128)(2,1)}, bf16[32,1,64,2048]{3,2,1,0:T(8,128)(2,1)S(1)}) fusion(bf16[32,2,64,2048]{3,2,1,0:T(8,128)(2,1)} %bitcast.23), kind=kLoop, calls=%fused_computation.65 | loop fusion | bytes 33554432 | tf_op jit(solution)/shard_map/slice | solution.py:96
  163.9 1.6 fusion.1
  166.5 3.7 %convolution_bitcast_fusion = f32[2048,256]{0,1:T(8,128)} fusion(bf16[256,2048]{1,0:T(8,128)(2,1)S(1)} %fusion.1, bf16[2048,2048]{1,0:T(8,128)(2,1)S(1)} %bitcast.25), kind=kOutput, calls=%fused_computation.2 | convolution fusion | flops 2147483648 | bytes 11534336 | tf_op jit(solution)/shard_map/dot_general | solution.py:97
  170.3 7.4 %convolution_bitcast_fusion.1 = f32[2048,256]{0,1:T(8,128)} fusion(bf16[256,2048]{1,0:T(8,128)(2,1)} %copy-done.7, bf16[2048,2048]{1,0:T(8,128)(2,1)} %bitcast.24), kind=kOutput, calls=%fused_computation.3 | convolution fusion | flops 2147483648 | bytes 11534336 | tf_op jit(solution)/shard_map/dot_general | solution.py:97
  179.5 29.7 %reduce-scatter.5.cloned.1.call-done = f32[256,256]{0,1:T(8,128)} async-done(((f32[2048,256]{0,1:T(8,128)}), f32[256,256]{0,1:T(8,128)}) %reduce-scatter.5.cloned.1.call-update) | async-done | bytes 262160 | tf_op jit(solution)/shard_map/reduce_scatter | solution.py:102
  210.2 2.2 collective-permute-start.10
  213.6 39.7 %reduce-scatter.3.cloned.1.call-done = f32[256,256]{0,1:T(8,128)} async-done(((f32[2048,256]{0,1:T(8,128)}), f32[256,256]{0,1:T(8,128)}) %reduce-scatter.3.cloned.1.call-update) | async-done | bytes 262160 | tf_op jit(solution)/shard_map/reduce_scatter | solution.py:102
  254.2 1.9 collective-permute-start.8
  257.1 1.8 collective-permute-start.11
  259.0 3.1 %collective-permute-done.8 = f32[128,256]{0,1:T(8,128)S(1)} collective-permute-done((f32[128,256]{0,1:T(8,128)S(1)}, f32[128,256]{0,1:T(8,128)S(1)}, u32[]{:S(2)}, u32[]{:S(2)}) %collective-permute-start.8) | collective-permute-done | bytes 131104 | tf_op jit(solution)/shard_map/ppermute | solution.py:33
  263.4 4.8 %collective-permute-done.9 = f32[64,256]{0,1:T(8,128)S(1)} collective-permute-done((f32[64,256]{0,1:T(8,128)S(1)}, f32[64,256]{0,1:T(8,128)S(1)}, u32[]{:S(2)}, u32[]{:S(2)}) %collective-permute-start.9) | collective-permute-done | bytes 65568 | tf_op jit(solution)/shard_map/ppermute | solution.py:33
  (64 shorter events, 15.5 us)
Async XLA Ops:
  7.2 92.6 %copy-start = (bf16[256,4096]{1,0:T(8,128)(2,1)S(1)}, bf16[256,4096]{1,0:T(8,128)(2,1)}, u32[]{:S(2)}) copy-start(bf16[256,4096]{1,0:T(8,128)(2,1)} %param.6) | copy-start | bytes 6291460
  7.2 0.8 copy-start.3
  7.2 92.6 %all-gather.2.cloned.1.call-start = ((), (), s32[]{:S(2)}) async-start(), calls=%async_computation.2 | async-start | bytes 18874368 | tf_op jit(solution)/shard_map/all_gather | solution.py:66
  7.9 201.4 %reduce-scatter.5.cloned.1.call-start = ((), (), s32[]{:S(2)}) async-start(), calls=%async_computation.4 | async-start | bytes 2359296 | tf_op jit(solution)/shard_map/reduce_scatter | solution.py:102
  107.9 11.5 %copy-start.5 = (f32[256,2048]{1,0:T(8,128)}, f32[256,2048]{1,0:T(8,128)S(1)}, u32[]{:S(2)}) copy-start(f32[256,2048]{1,0:T(8,128)S(1)} %fusion.34) | copy-start | bytes 6291460
  107.9 20.8 %copy-start.2 = (s32[2048]{0:T(1024)S(1)}, s32[2048]{0:T(1024)}, u32[]{:S(2)}) copy-start(s32[2048]{0:T(1024)} %param.11) | copy-start | bytes 24580
  108.0 22.1 %copy-start.1 = (f32[16,2048]{1,0:T(8,128)S(1)}, f32[16,2048]{1,0:T(8,128)}, u32[]{:S(2)}) copy-start(f32[16,2048]{1,0:T(8,128)} %param.8) | copy-start | bytes 393220
  109.2 1.6 collective-permute-start
  110.8 8.5 %collective-permute-start.1 = (f32[32,2048]{1,0:T(8,128)S(1)}, f32[32,2048]{1,0:T(8,128)S(1)}, u32[]{:S(2)}, u32[]{:S(2)}) collective-permute-start(f32[32,2048]{1,0:T(8,128)S(1)} %add.108), channel_id=1, source_target_pairs={{0,64},{64,0},{128,192},{192,128},{1,65},{65,1},{129,193},{193,129... | collective-permute-start | bytes 786440 | tf_op jit(solution)/shard_map/ppermute | solution.py:20
  119.4 9.2 %collective-permute-start.2 = (f32[32,2048]{1,0:T(8,128)S(1)}, f32[32,2048]{1,0:T(8,128)S(1)}, u32[]{:S(2)}, u32[]{:S(2)}) collective-permute-start(f32[32,2048]{1,0:T(8,128)S(1)} %add.109), channel_id=1, source_target_pairs={{0,128},{64,192},{128,0},{192,64},{1,129},{65,193},{129,1},{193,65... | collective-permute-start | bytes 786440 | tf_op jit(solution)/shard_map/ppermute | solution.py:20
  130.5 3.8 %collective-permute-start.3 = (f32[17,32]{1,0:T(8,128)S(1)}, f32[17,32]{1,0:T(8,128)S(1)}, u32[]{:S(2)}, u32[]{:S(2)}) collective-permute-start(f32[17,32]{1,0:T(8,128)S(1)} %pad_maximum_fusion), channel_id=1, source_target_pairs={{0,1},{1,0},{2,3},{3,2},{4,5},{5,4},{6,7},{7,6},{8,9},{9,8},{10,11... | collective-permute-start | bytes 6536 | tf_op jit(solution)/shard_map/ppermute | solution.py:20
  134.3 5.2 %collective-permute-start.4 = (f32[17,32]{1,0:T(8,128)S(1)}, f32[17,32]{1,0:T(8,128)S(1)}, u32[]{:S(2)}, u32[]{:S(2)}) collective-permute-start(f32[17,32]{1,0:T(8,128)S(1)} %fusion.32), channel_id=1, source_target_pairs={{0,2},{1,3},{2,0},{3,1},{4,6},{5,7},{6,4},{7,5},{8,10},{9,11},{10,... | collective-permute-start | bytes 6536 | tf_op jit(solution)/shard_map/ppermute | solution.py:20
  139.5 3.7 %collective-permute-start.5 = (f32[17,32]{1,0:T(8,128)S(1)}, f32[17,32]{1,0:T(8,128)S(1)}, u32[]{:S(2)}, u32[]{:S(2)}) collective-permute-start(f32[17,32]{1,0:T(8,128)S(1)} %add.114), channel_id=1, source_target_pairs={{0,4},{4,0},{8,12},{12,8},{16,20},{20,16},{24,28},{28,24},{1,5},{5... | collective-permute-start | bytes 6536 | tf_op jit(solution)/shard_map/ppermute | solution.py:20
  143.2 4.6 %collective-permute-start.6 = (f32[17,32]{1,0:T(8,128)S(1)}, f32[17,32]{1,0:T(8,128)S(1)}, u32[]{:S(2)}, u32[]{:S(2)}) collective-permute-start(f32[17,32]{1,0:T(8,128)S(1)} %add.115), channel_id=1, source_target_pairs={{0,8},{4,12},{8,0},{12,4},{16,24},{20,28},{24,16},{28,20},{1,9},{5... | collective-permute-start | bytes 6536 | tf_op jit(solution)/shard_map/ppermute | solution.py:20
  147.8 15.6 %collective-permute-start.7 = (f32[17,32]{1,0:T(8,128)S(1)}, f32[17,32]{1,0:T(8,128)S(1)}, u32[]{:S(2)}, u32[]{:S(2)}) collective-permute-start(f32[17,32]{1,0:T(8,128)S(1)} %add.116), channel_id=1, source_target_pairs={{0,16},{4,20},{8,24},{12,28},{16,0},{20,4},{24,8},{28,12},{1,17},{... | collective-permute-start | bytes 6536 | tf_op jit(solution)/shard_map/ppermute | solution.py:20
  153.5 9.9 %copy-start.4 = (s32[32]{0:T(128)S(1)}, s32[32]{0:T(128)}, u32[]{:S(2)}) copy-start(s32[32]{0:T(128)} %param.10) | copy-start | bytes 388
  153.5 10.4 %copy-start.6 = (f32[256,2048]{1,0:T(8,128)S(1)}, f32[256,2048]{1,0:T(8,128)}, u32[]{:S(2)}) copy-start(f32[256,2048]{1,0:T(8,128)} %copy-done.5) | copy-start | bytes 6291460
  165.6 1.0 copy-start.7
  170.2 83.1 %reduce-scatter.3.cloned.1.call-start = ((), (), s32[]{:S(2)}) async-start(), calls=%async_computation.3 | async-start | bytes 2359296 | tf_op jit(solution)/shard_map/reduce_scatter | solution.py:102
  210.2 45.9 %collective-permute-start.10 = (f32[128,256]{0,1:T(8,128)S(1)}, f32[128,256]{0,1:T(8,128)S(1)}, u32[]{:S(2)}, u32[]{:S(2)}) collective-permute-start(f32[128,256]{0,1:T(8,128)S(1)} %constant_dynamic-slice_fusion.1), channel_id=1, source_target_pairs={{0,2},{1,3},{2,0},{3,1},{4,6},{5,7},{6,4},{7,5},{8,10},{9,11},{10,... | collective-permute-start | bytes 393224 | tf_op jit(solution)/shard_map/ppermute | solution.py:33
  254.2 7.9 %collective-permute-start.8 = (f32[128,256]{0,1:T(8,128)S(1)}, f32[128,256]{0,1:T(8,128)S(1)}, u32[]{:S(2)}, u32[]{:S(2)}) collective-permute-start(f32[128,256]{0,1:T(8,128)S(1)} %constant_dynamic-slice_fusion.3), channel_id=1, source_target_pairs={{0,2},{1,3},{2,0},{3,1},{4,6},{5,7},{6,4},{7,5},{8,10},{9,11},{10,... | collective-permute-start | bytes 393224 | tf_op jit(solution)/shard_map/ppermute | solution.py:33
  257.1 6.1 %collective-permute-start.11 = (f32[64,256]{0,1:T(8,128)S(1)}, f32[64,256]{0,1:T(8,128)S(1)}, u32[]{:S(2)}, u32[]{:S(2)}) collective-permute-start(f32[64,256]{0,1:T(8,128)S(1)} %constant_dynamic-slice_fusion), channel_id=1, source_target_pairs={{0,1},{1,0},{2,3},{3,2},{4,5},{5,4},{6,7},{7,6},{8,9},{9,8},{10,11... | collective-permute-start | bytes 196616 | tf_op jit(solution)/shard_map/ppermute | solution.py:33
  263.2 5.1 %collective-permute-start.9 = (f32[64,256]{0,1:T(8,128)S(1)}, f32[64,256]{0,1:T(8,128)S(1)}, u32[]{:S(2)}, u32[]{:S(2)}) collective-permute-start(f32[64,256]{0,1:T(8,128)S(1)} %constant_dynamic-slice_fusion.2), channel_id=1, source_target_pairs={{0,1},{1,0},{2,3},{3,2},{4,5},{5,4},{6,7},{7,6},{8,9},{9,8},{10,11... | collective-permute-start | bytes 196616 | tf_op jit(solution)/shard_map/ppermute | solution.py:33
Sparse Core Ops, SparseCore 0:
  9.9 89.9 all-gather.1
  170.4 38.8 reduce-scatter.4
  211.8 41.4 reduce-scatter.2
where the time goes:
time: 276 us
  waiting for transfers between devices  197 us (71%)
  matrix products  22.8 us (8%)
  starting transfers between devices  21.3 us (8%)
  between operations  15.3 us (6%)
  local copies, waits for them, and re-layouts  13.5 us (5%)
  other arithmetic  5.73 us (2%)
    all_gather x1, waiting for transfers between devices, per_device(): full_head = lax.all_gather(head_weight, SEQ, axis=0, tiled=True)  91.5 us
    reduce_scatter x2, waiting for transfers between devices, per_device(): lax.psum_scatter(partial, 'vz', scatter_dimension=0, tiled=True)  69.4 us
    ppermute x8, waiting for transfers between devices, butterfly(): lax.ppermute(a, ax, [(i, i ^ d) for i in range(n)])  27.2 us
    ppermute x8, starting transfers between devices, butterfly(): lax.ppermute(a, ax, [(i, i ^ d) for i in range(n)])  15.2 us
    dot_general x2, matrix products, per_device(): lax.dot_general(rows, dlogits, (((1,), (1,)), ((), ())), preferred_elemen...  11.1 us
    slice x1, local copies, waits for them, and re-layouts, per_device(): rows = grouped[:, g].reshape(-1, vocab_cols)  9.88 us
    dot_general x1, matrix products, per_device(): logits = jnp.dot(hidden, full_head, preferred_element_type=jnp.float32)  8.11 us
    ppermute x4, waiting for transfers between devices, halving_scatter(): x = keep + lax.ppermute(send, ax, [(i, i ^ d) for i in range(n)])  7.99 us
  transfers between devices with their start and end apart: 15, of which 12 were waited for; matrix products, arithmetic and copies ran while one was open for 9% of the time, Pallas kernels for 0%

commit v1 on v0

--- a/solution.py
+++ b/solution.py
@@ -63,7 +63,9 @@
     counts = passage_lengths.astype(jnp.float32)
     weights_df = jnp.log(1.0 + DOCS / (1.0 + doc_freq.astype(jnp.float32)))
     flops_grad = loss_scale * flops_weight * 2.0 / (vocab_total * passages)
-    full_head = lax.all_gather(head_weight, SEQ, axis=0, tiled=True)
+    full_head = jnp.concatenate(
+        lax.all_to_all(jnp.stack([head_weight] * lax.axis_size(SEQ), 0), SEQ, 0, 0), 0
+    )
     logits = jnp.dot(hidden, full_head, preferred_element_type=jnp.float32)
     lifted = 1.0 + jax.nn.relu(logits)
     squared = lifted * lifted

time: 276 us -> 382 us (1.38)
  waiting for transfers between devices: 197 us -> 285 us
  starting transfers between devices: 21.3 us -> 31.7 us
  local copies, waits for them, and re-layouts: 13.5 us -> 20.6 us
    all_to_all x0 -> x1, waiting for transfers between devices: none -> 183 us  [per_device(): lax.all_to_all(jnp.stack([head_weight] * lax.axis_size(SEQ), 0), SEQ, 0, 0)]
    all_gather x1 -> x0, waiting for transfers between devices: 91.5 us -> none  [per_device(): full_head = lax.all_gather(head_weight, SEQ, axis=0, tiled=True)]
    another operation x1 -> x2, local copies, waits for them, and re-layouts: 0.09 us -> 7.14 us  [the longest x1 7.05 us: per_device(): jnp.stack([head_weight] * lax.axis_size(SEQ), 0)]
    all_to_all x0 -> x1, starting transfers between devices: none -> 6.29 us  [per_device(): lax.all_to_all(jnp.stack([head_weight] * lax.axis_size(SEQ), 0), SEQ, 0, 0)]
    ppermute x8, starting transfers between devices: 15.2 us -> 19.3 us  [butterfly(): lax.ppermute(a, ax, [(i, i ^ d) for i in range(n)])]
  transfers between devices with their start and end apart: 15 -> 15, of which waited for: 12 -> 12; matrix products, arithmetic and copies ran while one was open for 9% -> 6% of each run, Pallas kernels for 0% -> 0%
where the time goes in v1:
time: 382 us
  waiting for transfers between devices  285 us (75%)
  starting transfers between devices  31.7 us (8%)
  matrix products  22.8 us (6%)
  local copies, waits for them, and re-layouts  20.6 us (5%)
  between operations  15.6 us (4%)
  other arithmetic  5.73 us (2%)
    all_to_all x1, waiting for transfers between devices, per_device(): lax.all_to_all(jnp.stack([head_weight] * lax.axis_size(SEQ), 0), SEQ, 0, 0)  183 us
    reduce_scatter x2, waiting for transfers between devices, per_device(): lax.psum_scatter(partial, 'vz', scatter_dimension=0, tiled=True)  69.9 us
    ppermute x8, waiting for transfers between devices, butterfly(): lax.ppermute(a, ax, [(i, i ^ d) for i in range(n)])  24.3 us
    ppermute x8, starting transfers between devices, butterfly(): lax.ppermute(a, ax, [(i, i ^ d) for i in range(n)])  19.3 us
    dot_general x2, matrix products, per_device(): lax.dot_general(rows, dlogits, (((1,), (1,)), ((), ())), preferred_elemen...  11.1 us
    slice x1, local copies, waits for them, and re-layouts, per_device(): rows = grouped[:, g].reshape(-1, vocab_cols)  9.89 us
    dot_general x1, matrix products, per_device(): logits = jnp.dot(hidden, full_head, preferred_element_type=jnp.float32)  8.11 us
    ppermute x4, waiting for transfers between devices, halving_scatter(): x = keep + lax.ppermute(send, ax, [(i, i ^ d) for i in range(n)])  8.08 us
  transfers between devices with their start and end apart: 15, of which 12 were waited for; matrix products, arithmetic and copies ran while one was open for 6% of the time, Pallas kernels for 0%

profile of v1, /device:TPU:10, one launch (start us, length us, event | category | flops | bytes accessed | tf_op | source)
XLA Modules:
  0.0 381.5 jit_solution(11102339219579797799)
XLA Ops:
  7.2 7.0 %stack.6 = bf16[8,512,2048]{2,1,0:T(8,128)(2,1)} broadcast(bf16[512,2048]{1,0:T(8,128)(2,1)} %param.7), dimensions={1,2} | broadcast | bytes 18874368 | tf_op jit(solution)/shard_map/stack | solution.py:67
  14.2 6.3 %all-to-all-start = ((bf16[8,512,2048]{2,1,0:T(8,128)(2,1)}), bf16[8,512,2048]{2,1,0:T(8,128)(2,1)}, u32[]{:S(2)}, u32[]{:S(2)}) async-start(bf16[8,512,2048]{2,1,0:T(8,128)(2,1)} %stack.6), calls=%async_computation | async-start | bytes 33554432 | tf_op jit(solution)/shard_map/all_to_all | solution.py:67
  20.8 182.8 %all-to-all-done = bf16[8,512,2048]{2,1,0:T(8,128)(2,1)} async-done(((bf16[8,512,2048]{2,1,0:T(8,128)(2,1)}), bf16[8,512,2048]{2,1,0:T(8,128)(2,1)}, u32[]{:S(2)}, u32[]{:S(2)}) %all-to-all-start) | async-done | bytes 16777248 | tf_op jit(solution)/shard_map/all_to_all | solution.py:67
  203.7 8.1 %fusion.34 = f32[256,2048]{1,0:T(8,128)S(1)} fusion(bf16[256,4096]{1,0:T(8,128)(2,1)S(1)} %copy-done, bf16[4096,2048]{1,0:T(8,128)(2,1)} %bitcast), kind=kOutput, calls=%fused_computation.66 | convolution fusion | flops 4294967296 | bytes 20971520 | tf_op jit(solution)/shard_map/dot_general | solution.py:69
  216.2 6.9 %collective-permute-done.1 = f32[32,2048]{1,0:T(8,128)S(1)} collective-permute-done((f32[32,2048]{1,0:T(8,128)S(1)}, f32[32,2048]{1,0:T(8,128)S(1)}, u32[]{:S(2)}, u32[]{:S(2)}) %collective-permute-start.1) | collective-permute-done | bytes 262176 | tf_op jit(solution)/shard_map/ppermute | solution.py:20
  224.7 7.6 %collective-permute-done.2 = f32[32,2048]{1,0:T(8,128)S(1)} collective-permute-done((f32[32,2048]{1,0:T(8,128)S(1)}, f32[32,2048]{1,0:T(8,128)S(1)}, u32[]{:S(2)}, u32[]{:S(2)}) %collective-permute-start.2) | collective-permute-done | bytes 262176 | tf_op jit(solution)/shard_map/ppermute | solution.py:20
  234.1 2.2 collective-permute-start.3
  236.3 1.7 collective-permute-done.3
  238.0 2.2 collective-permute-start.4
  240.2 3.0 collective-permute-done.4
  243.2 1.8 collective-permute-start.5
  245.0 1.9 collective-permute-done.5
  246.9 3.1 collective-permute-start.6
  250.1 1.7 collective-permute-done.6
  251.7 6.8 %collective-permute-start.7 = (f32[17,32]{1,0:T(8,128)S(1)}, f32[17,32]{1,0:T(8,128)S(1)}, u32[]{:S(2)}, u32[]{:S(2)}) collective-permute-start(f32[17,32]{1,0:T(8,128)S(1)} %add.116), channel_id=1, source_target_pairs={{0,16},{4,20},{8,24},{12,28},{16,0},{20,4},{24,8},{28,12},{1,17},{... | collective-permute-start | bytes 6536 | tf_op jit(solution)/shard_map/ppermute | solution.py:20
  258.6 9.9 %fusion.33 = (bf16[32,1,64,2048]{3,2,1,0:T(8,128)(2,1)S(1)}, bf16[32,1,64,2048]{3,2,1,0:T(8,128)(2,1)}) fusion(bf16[32,2,64,2048]{3,2,1,0:T(8,128)(2,1)} %bitcast.3), kind=kLoop, calls=%fused_computation.65 | loop fusion | bytes 33554432 | tf_op jit(solution)/shard_map/slice | solution.py:98
  271.6 3.7 convolution_bitcast_fusion.1
  275.3 7.4 %convolution_bitcast_fusion = f32[2048,256]{0,1:T(8,128)} fusion(bf16[256,2048]{1,0:T(8,128)(2,1)} %copy-done.7, bf16[2048,2048]{1,0:T(8,128)(2,1)} %bitcast.24), kind=kOutput, calls=%fused_computation.2 | convolution fusion | flops 2147483648 | bytes 11534336 | tf_op jit(solution)/shard_map/dot_general | solution.py:99
  284.6 30.2 %reduce-scatter.3.cloned.1.call-done = f32[256,256]{0,1:T(8,128)} async-done(((f32[2048,256]{0,1:T(8,128)}), f32[256,256]{0,1:T(8,128)}) %reduce-scatter.3.cloned.1.call-update) | async-done | bytes 262160 | tf_op jit(solution)/shard_map/reduce_scatter | solution.py:104
  315.8 2.2 collective-permute-start.8
  319.2 39.7 %reduce-scatter.5.cloned.1.call-done = f32[256,256]{0,1:T(8,128)} async-done(((f32[2048,256]{0,1:T(8,128)}), f32[256,256]{0,1:T(8,128)}) %reduce-scatter.5.cloned.1.call-update) | async-done | bytes 262160 | tf_op jit(solution)/shard_map/reduce_scatter | solution.py:104
  359.8 2.2 collective-permute-start.10
  364.5 3.2 collective-permute-done.10
  369.0 4.8 %collective-permute-done.11 = f32[64,256]{0,1:T(8,128)S(1)} collective-permute-done((f32[64,256]{0,1:T(8,128)S(1)}, f32[64,256]{0,1:T(8,128)S(1)}, u32[]{:S(2)}, u32[]{:S(2)}) %collective-permute-start.11) | collective-permute-done | bytes 65568 | tf_op jit(solution)/shard_map/ppermute | solution.py:33
  (64 shorter events, 19.3 us)
Async XLA Ops:
  7.2 196.5 %copy-start = (bf16[256,4096]{1,0:T(8,128)(2,1)S(1)}, bf16[256,4096]{1,0:T(8,128)(2,1)}, u32[]{:S(2)}) copy-start(bf16[256,4096]{1,0:T(8,128)(2,1)} %param.6) | copy-start | bytes 6291460
  14.2 6.3 %copy-start.3 = (s32[32]{0:T(128)S(1)}, s32[32]{0:T(128)}, u32[]{:S(2)}) copy-start(s32[32]{0:T(128)} %param.9) | copy-start | bytes 388
  14.2 189.4 %all-to-all-start = ((bf16[8,512,2048]{2,1,0:T(8,128)(2,1)}), bf16[8,512,2048]{2,1,0:T(8,128)(2,1)}, u32[]{:S(2)}, u32[]{:S(2)}) async-start(bf16[8,512,2048]{2,1,0:T(8,128)(2,1)} %stack.6), calls=%async_computation | async-start | bytes 33554432 | tf_op jit(solution)/shard_map/all_to_all | solution.py:67
  20.5 294.3 %reduce-scatter.3.cloned.1.call-start = ((), (), s32[]{:S(2)}) async-start(), calls=%async_computation.3 | async-start | bytes 2359296 | tf_op jit(solution)/shard_map/reduce_scatter | solution.py:104
  211.8 11.4 %copy-start.5 = (f32[256,2048]{1,0:T(8,128)}, f32[256,2048]{1,0:T(8,128)S(1)}, u32[]{:S(2)}) copy-start(f32[256,2048]{1,0:T(8,128)S(1)} %fusion.34) | copy-start | bytes 6291460
  211.8 20.6 %copy-start.2 = (s32[2048]{0:T(1024)S(1)}, s32[2048]{0:T(1024)}, u32[]{:S(2)}) copy-start(s32[2048]{0:T(1024)} %param.11) | copy-start | bytes 24580
  211.8 21.9 %copy-start.1 = (f32[16,2048]{1,0:T(8,128)S(1)}, f32[16,2048]{1,0:T(8,128)}, u32[]{:S(2)}) copy-start(f32[16,2048]{1,0:T(8,128)} %param.8) | copy-start | bytes 393220
  213.0 1.6 collective-permute-start
  214.7 8.4 %collective-permute-start.1 = (f32[32,2048]{1,0:T(8,128)S(1)}, f32[32,2048]{1,0:T(8,128)S(1)}, u32[]{:S(2)}, u32[]{:S(2)}) collective-permute-start(f32[32,2048]{1,0:T(8,128)S(1)} %add.108), channel_id=1, source_target_pairs={{0,64},{64,0},{128,192},{192,128},{1,65},{65,1},{129,193},{193,129... | collective-permute-start | bytes 786440 | tf_op jit(solution)/shard_map/ppermute | solution.py:20
  223.2 9.1 %collective-permute-start.2 = (f32[32,2048]{1,0:T(8,128)S(1)}, f32[32,2048]{1,0:T(8,128)S(1)}, u32[]{:S(2)}, u32[]{:S(2)}) collective-permute-start(f32[32,2048]{1,0:T(8,128)S(1)} %add.109), channel_id=1, source_target_pairs={{0,128},{64,192},{128,0},{192,64},{1,129},{65,193},{129,1},{193,65... | collective-permute-start | bytes 786440 | tf_op jit(solution)/shard_map/ppermute | solution.py:20
  234.1 3.9 %collective-permute-start.3 = (f32[17,32]{1,0:T(8,128)S(1)}, f32[17,32]{1,0:T(8,128)S(1)}, u32[]{:S(2)}, u32[]{:S(2)}) collective-permute-start(f32[17,32]{1,0:T(8,128)S(1)} %pad_maximum_fusion), channel_id=1, source_target_pairs={{0,1},{1,0},{2,3},{3,2},{4,5},{5,4},{6,7},{7,6},{8,9},{9,8},{10,11... | collective-permute-start | bytes 6536 | tf_op jit(solution)/shard_map/ppermute | solution.py:20
  238.0 5.2 %collective-permute-start.4 = (f32[17,32]{1,0:T(8,128)S(1)}, f32[17,32]{1,0:T(8,128)S(1)}, u32[]{:S(2)}, u32[]{:S(2)}) collective-permute-start(f32[17,32]{1,0:T(8,128)S(1)} %fusion.32), channel_id=1, source_target_pairs={{0,2},{1,3},{2,0},{3,1},{4,6},{5,7},{6,4},{7,5},{8,10},{9,11},{10,... | collective-permute-start | bytes 6536 | tf_op jit(solution)/shard_map/ppermute | solution.py:20
  243.2 3.7 collective-permute-start.5
  246.9 4.8 %collective-permute-start.6 = (f32[17,32]{1,0:T(8,128)S(1)}, f32[17,32]{1,0:T(8,128)S(1)}, u32[]{:S(2)}, u32[]{:S(2)}) collective-permute-start(f32[17,32]{1,0:T(8,128)S(1)} %add.115), channel_id=1, source_target_pairs={{0,8},{4,12},{8,0},{12,4},{16,24},{20,28},{24,16},{28,20},{1,9},{5... | collective-permute-start | bytes 6536 | tf_op jit(solution)/shard_map/ppermute | solution.py:20
  251.7 16.7 %collective-permute-start.7 = (f32[17,32]{1,0:T(8,128)S(1)}, f32[17,32]{1,0:T(8,128)S(1)}, u32[]{:S(2)}, u32[]{:S(2)}) collective-permute-start(f32[17,32]{1,0:T(8,128)S(1)} %add.116), channel_id=1, source_target_pairs={{0,16},{4,20},{8,24},{12,28},{16,0},{20,4},{24,8},{28,12},{1,17},{... | collective-permute-start | bytes 6536 | tf_op jit(solution)/shard_map/ppermute | solution.py:20
  258.6 9.9 %copy-start.4 = (s32[32]{0:T(128)S(1)}, s32[32]{0:T(128)}, u32[]{:S(2)}) copy-start(s32[32]{0:T(128)} %param.10) | copy-start | bytes 388
  258.6 10.4 %copy-start.6 = (f32[256,2048]{1,0:T(8,128)S(1)}, f32[256,2048]{1,0:T(8,128)}, u32[]{:S(2)}) copy-start(f32[256,2048]{1,0:T(8,128)} %copy-done.5) | copy-start | bytes 6291460
  270.6 1.0 copy-start.7
  275.3 83.6 %reduce-scatter.5.cloned.1.call-start = ((), (), s32[]{:S(2)}) async-start(), calls=%async_computation.4 | async-start | bytes 2359296 | tf_op jit(solution)/shard_map/reduce_scatter | solution.py:104
  315.8 46.3 %collective-permute-start.8 = (f32[128,256]{0,1:T(8,128)S(1)}, f32[128,256]{0,1:T(8,128)S(1)}, u32[]{:S(2)}, u32[]{:S(2)}) collective-permute-start(f32[128,256]{0,1:T(8,128)S(1)} %constant_dynamic-slice_fusion.3), channel_id=1, source_target_pairs={{0,2},{1,3},{2,0},{3,1},{4,6},{5,7},{6,4},{7,5},{8,10},{9,11},{10,... | collective-permute-start | bytes 393224 | tf_op jit(solution)/shard_map/ppermute | solution.py:33
  359.8 7.9 %collective-permute-start.10 = (f32[128,256]{0,1:T(8,128)S(1)}, f32[128,256]{0,1:T(8,128)S(1)}, u32[]{:S(2)}, u32[]{:S(2)}) collective-permute-start(f32[128,256]{0,1:T(8,128)S(1)} %constant_dynamic-slice_fusion.1), channel_id=1, source_target_pairs={{0,2},{1,3},{2,0},{3,1},{4,6},{5,7},{6,4},{7,5},{8,10},{9,11},{10,... | collective-permute-start | bytes 393224 | tf_op jit(solution)/shard_map/ppermute | solution.py:33
  363.0 5.9 %collective-permute-start.9 = (f32[64,256]{0,1:T(8,128)S(1)}, f32[64,256]{0,1:T(8,128)S(1)}, u32[]{:S(2)}, u32[]{:S(2)}) collective-permute-start(f32[64,256]{0,1:T(8,128)S(1)} %constant_dynamic-slice_fusion.2), channel_id=1, source_target_pairs={{0,1},{1,0},{2,3},{3,2},{4,5},{5,4},{6,7},{7,6},{8,9},{9,8},{10,11... | collective-permute-start | bytes 196616 | tf_op jit(solution)/shard_map/ppermute | solution.py:33
  368.8 5.1 %collective-permute-start.11 = (f32[64,256]{0,1:T(8,128)S(1)}, f32[64,256]{0,1:T(8,128)S(1)}, u32[]{:S(2)}, u32[]{:S(2)}) collective-permute-start(f32[64,256]{0,1:T(8,128)S(1)} %constant_dynamic-slice_fusion), channel_id=1, source_target_pairs={{0,1},{1,0},{2,3},{3,2},{4,5},{5,4},{6,7},{7,6},{8,9},{9,8},{10,11... | collective-permute-start | bytes 196616 | tf_op jit(solution)/shard_map/ppermute | solution.py:33
Sparse Core Ops, SparseCore 0:
  275.4 39.3 reduce-scatter.2
  317.4 41.4 reduce-scatter.4
